TPU v7x, 32 devices: a whole 2x2x4 slice. The times are simulated.
32 devices in a mesh: rows: 8 (over z, y), sub: 4 (over x, core).
Axes of the slice: x: 2, y: 2, z: 4, core: 2. Of those that a mesh axis runs over, the one named last changes fastest.
Arguments:
- held: float32 [512, 4, 128, 256], P('rows', 'sub'), may hold values from -256 to 256
- held_block: int32 [512, 4], P('rows', 'sub'), may hold values from 0 to 255, as said below
- held_count: int32 [8, 4], P('rows', 'sub'), may hold values from 0 to 64
Outputs:
- q_factor: float32 [256, 4, 128, 256], P('rows', 'sub')
- r_factor: float32 [256, 256], replicated
Inputs may be any that keep to these rules, and one draw needn't show every extreme that they name: `held_block`: for slots j < held_count of a device, the ids are block numbers of its column group; over all devices of a column group each block is held in exactly one such slot. Slots at or past held_count hold arbitrary ids and data. A device holds at most 8 blocks whose number b has b // 32 equal to any one given device index along rows, and some device reaches that.
All inputs are finite; a program needn't handle non-finite values.
Results may differ from a plain program's by a relative error of at most 0.0003.
Values sent between devices are 32-bit elements; how exact they have to be, the bound alone decides.
No kernel may reach another device: no remote copies, remote signals or barrier semaphores. Data moves between devices by JAX's collectives and lax.ppermute only.
A program may use at most 128 MiB of HBM per device.

v0:
```python
import jax
import jax.numpy as jnp
from jax import lax
from jax.sharding import PartitionSpec as P

BLK_DEV = 32


def factor(gram):
    lower = jnp.linalg.cholesky(gram)
    identity = jnp.eye(gram.shape[0], dtype=gram.dtype)
    inverse = lax.linalg.triangular_solve(lower, identity, left_side=True, lower=True)
    return (lower, inverse)


def gram_of(flattened, total):
    return (
        lax.dot_general(
            flattened,
            flattened,
            (((0,), (0,)), ((), ())),
            precision=lax.Precision.HIGHEST,
            preferred_element_type=jnp.float32,
        )
        / total
    )


def apply_inverse(flattened, inverse):
    return jnp.dot(
        flattened, inverse.T, precision=lax.Precision.HIGHEST, preferred_element_type=jnp.float32
    )


def reduce_gram(partial_value):
    return lax.psum(partial_value, ("rows", "sub"))


def per_device(held, held_block, held_count):
    capacity = held.shape[0]
    block_rows = held.shape[2]
    width = held.shape[3]
    devices_rows = lax.axis_size("rows")
    own_index = lax.axis_index("rows")
    per_slot = max(1, capacity // devices_rows)
    total = float(devices_rows * lax.axis_size("sub") * BLK_DEV * block_rows)
    blocks = held[:, 0]
    block_ids = held_block[:, 0]
    count = held_count[0, 0]
    slots = jnp.arange(capacity, dtype=jnp.int32)
    valid = slots < count
    destination = block_ids // BLK_DEV
    earlier = (
        (destination[:, None] == destination[None, :])
        & valid[None, :]
        & (slots[None, :] < slots[:, None])
    )
    rank_within = jnp.sum(earlier.astype(jnp.int32), axis=1)
    target = jnp.where(valid, destination * per_slot + rank_within, devices_rows * per_slot)
    labels_out = block_ids.astype(jnp.float32)
    outgoing = (
        jnp.zeros((devices_rows * per_slot, block_rows, width), jnp.float32)
        .at[target]
        .set(blocks, mode="drop")
    )
    labels = (
        jnp.full((devices_rows * per_slot,), -1.0, jnp.float32)
        .at[target]
        .set(labels_out, mode="drop")
    )
    arrived = lax.all_to_all(outgoing, "rows", split_axis=0, concat_axis=0, tiled=True)
    arrived_labels = lax.all_to_all(labels, "rows", split_axis=0, concat_axis=0, tiled=True)
    local = arrived_labels.astype(jnp.int32) - own_index * BLK_DEV
    place = jnp.where(arrived_labels >= 0.0, local, BLK_DEV)
    resident = (
        jnp.zeros((BLK_DEV, block_rows, width), jnp.float32).at[place].set(arrived, mode="drop")
    )
    flattened = resident.reshape(-1, width)
    partial_one = gram_of(flattened, total)
    lower_one, inverse_one = factor(reduce_gram(partial_one))
    first = apply_inverse(flattened, inverse_one)
    lower_two, inverse_two = factor(reduce_gram(gram_of(first, total)))
    second, lower_one, lower_two = (apply_inverse(first, inverse_two), lower_one, lower_two)
    result = second.reshape(BLK_DEV, block_rows, width)
    r_factor = jnp.dot(
        lower_two.T,
        lower_one.T,
        precision=lax.Precision.HIGHEST,
        preferred_element_type=jnp.float32,
    )
    return (result[:, None], r_factor)


def solution(mesh):
    in_specs = (P("rows", "sub", None, None), P("rows", "sub"), P("rows", "sub"))
    out_specs = (P("rows", "sub", None, None), P())
    return jax.shard_map(
        per_device, mesh=mesh, in_specs=in_specs, out_specs=out_specs, check_vma=False
    )
```

profile of v0, /device:TPU:0, one launch (start us, length us, event | category | flops | bytes accessed | tf_op | source)
XLA Modules:
  0.0 661.4 jit_solution(13611043332102278474)
XLA Ops:
  10.8 7.3 %all-to-all-start = ((f32[8,8,1]{1,2,0:T(1,128)}), f32[8,8,1]{1,2,0:T(1,128)S(1)}, u32[]{:S(2)}, u32[]{:S(2)}) async-start(f32[8,8,1]{1,2,0:T(1,128)} %bitcast.5), calls=%async_computation | async-start | bytes 8192 | tf_op jit(solution)/shard_map/all_to_all | solution.py:72
  18.1 4.2 broadcast_in_dim.26
  22.3 15.6 %scatter_fusion = f32[64,128,256]{2,1,0:T(8,128)} fusion(f32[64,128,256]{2,1,0:T(8,128)} %broadcast_in_dim.26, s32[64]{0:T(128)S(1)} %fusion.38, f32[64,128,256]{2,1,0:T(8,128)} %bitcast.102), kind=kCustom, calls=%fused_computation.1 | custom fusion | bytes 25166080 | tf_op jit(solution)/shard_map/scatter | solution.py:64
  38.0 6.3 all-to-all-start.1
  44.5 182.2 %all-to-all-done.1 = f32[64,128,256]{2,1,0:T(8,128)} async-done(((f32[64,128,256]{2,1,0:T(8,128)}), f32[64,128,256]{2,1,0:T(8,128)}, u32[]{:S(2)}, u32[]{:S(2)}) %all-to-all-start.1) | async-done | bytes 8388640 | tf_op jit(solution)/shard_map/all_to_all | solution.py:71
  226.6 2.5 broadcast_in_dim.11
  229.1 15.6 %scatter_fusion.1 = f32[32,128,256]{2,1,0:T(8,128)} fusion(f32[32,128,256]{2,1,0:T(8,128)} %broadcast_in_dim.11, s32[64]{0:T(128)S(1)} %fusion.37, f32[64,128,256]{2,1,0:T(8,128)} %all-to-all-done.1), kind=kCustom, calls=%fused_computation.2 | custom fusion | bytes 25166080 | tf_op jit(solution)/shard_map/scatter | solution.py:76
  244.8 10.9 %fusion = f32[256,256]{0,1:T(8,128)} fusion(f32[32,128,256]{2,1,0:T(8,128)} %scatter_fusion.1), kind=kOutput, calls=%fused_computation.9 | convolution fusion | flops 3221291008 | bytes 4456448 | tf_op jit(solution)/shard_map/dot_general | solution.py:18
  256.2 123.8 %all-reduce.4.cloned.1.call-done = f32[256,256]{0,1:T(8,128)} async-done(((f32[256,256]{0,1:T(8,128)}), f32[256,256]{0,1:T(8,128)}) %all-reduce.4.cloned.1.call-update) | async-done | bytes 262160 | tf_op jit(solution)/shard_map/psum | solution.py:36
  380.0 1.1 copy.27
  381.1 1.0 fusion.10
  382.1 11.7 %cholesky.130 = f32[128,128]{1,0:T(8,128)S(1)} custom-call(f32[128,128]{1,0:T(8,128)S(1)} %cholesky.194), custom_call_target="Cholesky" | custom-call | tf_op jit(solution)/shard_map/jit(cholesky)/cholesky | solution.py:10
  393.9 9.8 %custom-call.13 = f32[1,128,128]{1,2,0:T(8,128)S(1)} custom-call(f32[1,128,128]{2,1,0:T(8,128)S(1)} %get-tuple-element.55), custom_call_target="InvertDiagBlocksLowerTriangular" | custom-call | tf_op jit(solution)/shard_map/jit(cholesky)/cholesky | solution.py:10
  404.2 11.7 %cholesky.147 = f32[128,128]{1,0:T(8,128)S(1)} custom-call(f32[128,128]{1,0:T(8,128)S(1)} %convolution_subtract_fusion.3), custom_call_target="Cholesky" | custom-call | tf_op jit(solution)/shard_map/jit(cholesky)/cholesky | solution.py:10
  418.1 4.1 while.4
  418.8 1.4 bitcast_dynamic-update-slice_fusion.4
  420.8 1.4 bitcast_dynamic-update-slice_fusion.4
  422.3 19.7 %custom-call.14 = f32[2,128,128]{1,2,0:T(8,128)S(1)} custom-call(f32[2,128,128]{2,1,0:T(8,128)S(1)} %get-tuple-element.18), custom_call_target="InvertDiagBlocksLowerTriangular" | custom-call | tf_op jit(solution)/shard_map/triangular_solve/custom-call.0 | solution.py:12
  442.8 5.5 fusion.1
  448.3 1.9 copy-done
  450.2 7.4 %convolution_multiply_fusion = f32[256,256]{0,1:T(8,128)} fusion(f32[4096,256]{1,0:T(8,128)S(1)} %fusion.1), kind=kOutput, calls=%fused_computation.7 | convolution fusion | flops 3221291008 | bytes 4456448 | tf_op jit(solution)/shard_map/dot_general | solution.py:18
  457.7 124.2 %all-reduce.6.cloned.1.call-done = f32[256,256]{0,1:T(8,128)} async-done(((f32[256,256]{0,1:T(8,128)}), f32[256,256]{0,1:T(8,128)}) %all-reduce.6.cloned.1.call-update) | async-done | bytes 262160 | tf_op jit(solution)/shard_map/psum | solution.py:36
  581.9 1.1 copy.29
  584.0 11.7 %cholesky.164 = f32[128,128]{1,0:T(8,128)S(1)} custom-call(f32[128,128]{1,0:T(8,128)S(1)} %cholesky.197), custom_call_target="Cholesky" | custom-call | tf_op jit(solution)/shard_map/jit(cholesky)/cholesky | solution.py:10
  595.7 10.0 %custom-call.15 = f32[1,128,128]{1,2,0:T(8,128)S(1)} custom-call(f32[1,128,128]{2,1,0:T(8,128)S(1)} %get-tuple-element.51), custom_call_target="InvertDiagBlocksLowerTriangular" | custom-call | tf_op jit(solution)/shard_map/jit(cholesky)/cholesky | solution.py:10
  606.2 11.7 %cholesky.181 = f32[128,128]{1,0:T(8,128)S(1)} custom-call(f32[128,128]{1,0:T(8,128)S(1)} %convolution_subtract_fusion.2), custom_call_target="Cholesky" | custom-call | tf_op jit(solution)/shard_map/jit(cholesky)/cholesky | solution.py:10
  620.5 1.2 fusion.15
  621.8 3.9 while.5
  622.4 1.4 bitcast_dynamic-update-slice_fusion.5
  624.4 1.4 bitcast_dynamic-update-slice_fusion.5
  625.8 19.9 %custom-call.16 = f32[2,128,128]{1,2,0:T(8,128)S(1)} custom-call(f32[2,128,128]{2,1,0:T(8,128)S(1)} %get-tuple-element.19), custom_call_target="InvertDiagBlocksLowerTriangular" | custom-call | tf_op jit(solution)/shard_map/triangular_solve/custom-call.0 | solution.py:12
  646.6 7.7 %fusion.5 = f32[4096,256]{1,0:T(8,128)} fusion(f32[4096,256]{1,0:T(8,128)} %copy-done, f32[128,256]{1,0:T(8,128)S(1)} %fusion.26, f32[128,256]{1,0:T(8,128)S(1)} %fusion.21), kind=kOutput, calls=%fused_computation.18 | convolution fusion | flops 3221291008 | bytes 8650752 | tf_op jit(solution)/shard_map/dot_general | solution.py:30
  (53 shorter events, 12.1 us)
Async XLA Ops:
  10.8 27.1 %all-to-all-start = ((f32[8,8,1]{1,2,0:T(1,128)}), f32[8,8,1]{1,2,0:T(1,128)S(1)}, u32[]{:S(2)}, u32[]{:S(2)}) async-start(f32[8,8,1]{1,2,0:T(1,128)} %bitcast.5), calls=%async_computation | async-start | bytes 8192 | tf_op jit(solution)/shard_map/all_to_all | solution.py:72
  38.0 188.7 %all-to-all-start.1 = ((f32[64,128,256]{2,1,0:T(8,128)}), f32[64,128,256]{2,1,0:T(8,128)}, u32[]{:S(2)}, u32[]{:S(2)}) async-start(f32[64,128,256]{2,1,0:T(8,128)} %scatter_fusion), calls=%async_computation.1 | async-start | bytes 16777216 | tf_op jit(solution)/shard_map/all_to_all | solution.py:71
  44.3 335.7 %all-reduce.4.cloned.1.call-start = ((), (), s32[]{:S(2)}) async-start(), calls=%async_computation.2 | async-start | bytes 524288 | tf_op jit(solution)/shard_map/psum | solution.py:36
  255.7 326.2 %all-reduce.6.cloned.1.call-start = ((), (), s32[]{:S(2)}) async-start(), calls=%async_computation.3 | async-start | bytes 524288 | tf_op jit(solution)/shard_map/psum | solution.py:36
  448.3 1.9 copy-start
Sparse Core Ops, SparseCore 0:
  255.8 124.2 all-reduce.3
  457.8 123.9 all-reduce.5
where the time goes:
time: 669 us; the launch traced here: 661 us
  waiting for transfers between devices  430 us (64%)
  other arithmetic  112 us (17%)
  local copies, waits for them, and re-layouts  51.7 us (8%)
  matrix products  35.4 us (5%)
  between operations  17.9 us (3%)
  starting transfers between devices  14.2 us (2%)
    psum x2, waiting for transfers between devices, reduce_gram(): return lax.psum(partial_value, ('rows', 'sub'))  248 us
    all_to_all x1, waiting for transfers between devices, per_device(): lax.all_to_all(outgoing, 'rows', split_axis=0, concat_axis=0, tiled=True)  182 us
    another operation x13, other arithmetic, factor(): lower = jnp.linalg.cholesky(gram)  68.8 us
    another operation x5, other arithmetic, factor(): lax.linalg.triangular_solve(lower, identity, left_side=True, lower=True)  39.7 us
    dot_general x2, matrix products, gram_of(): lax.dot_general(flattened, flattened, (((0,), (0,)), ((), ())), precision...  18.3 us
    scatter x1, local copies, waits for them, and re-layouts, per_device(): jnp.zeros((BLK_DEV, block_rows, width), jnp.float32).at[place]  15.6 us
    scatter x1, local copies, waits for them, and re-layouts, per_device(): outgoing = jnp.zeros((devices_rows * per_slot, block_rows, width), jnp.fl...  15.6 us
  transfers between devices with their start and end apart: 4, of which 3 were waited for; matrix products, arithmetic and copies ran while one was open for 3% of the time, Pallas kernels for 0%

commit v1 on v0

--- a/solution.py
+++ b/solution.py
@@ -32,8 +32,36 @@
     )
 
 
+def _xor_pairs(n, bit):
+    return [(i, i ^ bit) for i in range(n)]
+
+
+def _power_of_two(n):
+    return n > 0 and (n & (n - 1)) == 0
+
+
 def reduce_gram(partial_value):
-    return lax.psum(partial_value, ("rows", "sub"))
+    n_sub = lax.axis_size("sub")
+    n_rows = lax.axis_size("rows")
+    width = partial_value.shape[0]
+    if not (_power_of_two(n_sub) and _power_of_two(n_rows) and n_sub >= 2 and width % 2 == 0):
+        return lax.psum(partial_value, ("rows", "sub"))
+    x = partial_value + lax.ppermute(partial_value, "sub", _xor_pairs(n_sub, 1))
+    half = width // 2
+    h = lax.axis_index("sub") % 2
+    y = lax.dynamic_slice_in_dim(x, h * half, half, 0)
+    bit = 2
+    while bit < n_sub:
+        y = y + lax.ppermute(y, "sub", _xor_pairs(n_sub, bit))
+        bit *= 2
+    bit = 1
+    while bit < n_rows:
+        y = y + lax.ppermute(y, "rows", _xor_pairs(n_rows, bit))
+        bit *= 2
+    other = lax.ppermute(y, "sub", _xor_pairs(n_sub, 1))
+    first_half = jnp.where(h == 0, y, other)
+    second_half = jnp.where(h == 0, other, y)
+    return jnp.concatenate([first_half, second_half], axis=0)
 
 
 def per_device(held, held_block, held_count):
@@ -43,12 +71,14 @@
     devices_rows = lax.axis_size("rows")
     own_index = lax.axis_index("rows")
     per_slot = max(1, capacity // devices_rows)
+    n_out = devices_rows * per_slot
     total = float(devices_rows * lax.axis_size("sub") * BLK_DEV * block_rows)
     blocks = held[:, 0]
     block_ids = held_block[:, 0]
     count = held_count[0, 0]
     slots = jnp.arange(capacity, dtype=jnp.int32)
     valid = slots < count
+
     destination = block_ids // BLK_DEV
     earlier = (
         (destination[:, None] == destination[None, :])
@@ -56,31 +86,27 @@
         & (slots[None, :] < slots[:, None])
     )
     rank_within = jnp.sum(earlier.astype(jnp.int32), axis=1)
-    target = jnp.where(valid, destination * per_slot + rank_within, devices_rows * per_slot)
-    labels_out = block_ids.astype(jnp.float32)
-    outgoing = (
-        jnp.zeros((devices_rows * per_slot, block_rows, width), jnp.float32)
-        .at[target]
-        .set(blocks, mode="drop")
-    )
-    labels = (
-        jnp.full((devices_rows * per_slot,), -1.0, jnp.float32)
-        .at[target]
-        .set(labels_out, mode="drop")
-    )
+    target = jnp.where(valid, destination * per_slot + rank_within, n_out)
+    positions = jnp.arange(n_out, dtype=jnp.int32)
+    match = target[None, :] == positions[:, None]
+    source = jnp.sum(jnp.where(match, slots[None, :], 0), axis=1)
+    present = jnp.any(match, axis=1)
+    labels = jnp.where(present, jnp.take(block_ids, source), -1).astype(jnp.int32)
+    outgoing = jnp.take(blocks, source, axis=0)
     arrived = lax.all_to_all(outgoing, "rows", split_axis=0, concat_axis=0, tiled=True)
     arrived_labels = lax.all_to_all(labels, "rows", split_axis=0, concat_axis=0, tiled=True)
-    local = arrived_labels.astype(jnp.int32) - own_index * BLK_DEV
-    place = jnp.where(arrived_labels >= 0.0, local, BLK_DEV)
-    resident = (
-        jnp.zeros((BLK_DEV, block_rows, width), jnp.float32).at[place].set(arrived, mode="drop")
-    )
-    flattened = resident.reshape(-1, width)
-    partial_one = gram_of(flattened, total)
-    lower_one, inverse_one = factor(reduce_gram(partial_one))
-    first = apply_inverse(flattened, inverse_one)
-    lower_two, inverse_two = factor(reduce_gram(gram_of(first, total)))
-    second, lower_one, lower_two = (apply_inverse(first, inverse_two), lower_one, lower_two)
+
+    masked = jnp.where(valid[:, None, None], blocks, 0.0).reshape(-1, width)
+    lower_one, inverse_one = factor(reduce_gram(gram_of(masked, total)))
+    first_held = apply_inverse(masked, inverse_one)
+    lower_two, inverse_two = factor(reduce_gram(gram_of(first_held, total)))
+
+    wanted = own_index * BLK_DEV + jnp.arange(BLK_DEV, dtype=jnp.int32)
+    hit = arrived_labels[None, :] == wanted[:, None]
+    place = jnp.sum(jnp.where(hit, positions[None, :], 0), axis=1)
+    resident = jnp.take(arrived, place, axis=0).reshape(-1, width)
+    first = apply_inverse(resident, inverse_one)
+    second = apply_inverse(first, inverse_two)
     result = second.reshape(BLK_DEV, block_rows, width)
     r_factor = jnp.dot(
         lower_two.T,

time: 669 us -> 433 us (0.65)
  waiting for transfers between devices: 430 us -> 173 us
  matrix products: 35.4 us -> 64.6 us
  local copies, waits for them, and re-layouts: 51.7 us -> 24.3 us
  other arithmetic: 112 us -> 132 us
  between operations: 17.9 us -> 4.58 us
  starting transfers between devices: 14.2 us -> 26 us
    psum x2 -> x0, waiting for transfers between devices: 248 us -> none  [reduce_gram(): return lax.psum(partial_value, ('rows', 'sub'))]
    all_to_all x1, waiting for transfers between devices: 182 us -> 0.01 us  [per_device(): lax.all_to_all(outgoing, 'rows', split_axis=0, concat_axis=0, tiled=True)]
    ppermute x0 -> x12, waiting for transfers between devices: none -> 173 us  [the longest x6 160 us: reduce_gram(): y = y + lax.ppermute(y, 'rows', _xor_pairs(n_rows, bit))]
    scatter x3 -> x0, local copies, waits for them, and re-layouts: 32 us -> none  [the longest x1 15.6 us: per_device(): jnp.zeros((BLK_DEV, block_rows, width), jnp.float32).at[place]]
    select_n x3 -> x9, other arithmetic: 0.04 us -> 21.4 us  [the longest x1 8.3 us: per_device(): outgoing = jnp.take(blocks, source, axis=0)]
    gather x0 -> x4, local copies, waits for them, and re-layouts: none -> 15.4 us  [the longest x1 7.69 us: per_device(): outgoing = jnp.take(blocks, source, axis=0)]
    dot_general x2, matrix products: 18.3 us -> 33.5 us  [gram_of(): lax.dot_general(flattened, flattened, (((0,), (0,)), ((), ())), precision...]
    dot_general x2 -> x3, matrix products: 13.1 us -> 27.2 us  [apply_inverse(): jnp.dot(flattened, inverse.T, precision=lax.Precision.HIGHEST, preferred_...]
  transfers between devices with their start and end apart: 4 -> 14, of which waited for: 3 -> 12; matrix products, arithmetic and copies ran while one was open for 3% -> 46% of each run, Pallas kernels for 0% -> 0%
where the time goes in v1:
time: 433 us; the launch traced here: 425 us
  waiting for transfers between devices  173 us (40%)
  other arithmetic  132 us (30%)
  matrix products  64.6 us (15%)
  starting transfers between devices  26 us (6%)
  local copies, waits for them, and re-layouts  24.3 us (6%)
  between operations  4.58 us (1%)
    ppermute x6, waiting for transfers between devices, reduce_gram(): y = y + lax.ppermute(y, 'rows', _xor_pairs(n_rows, bit))  160 us
    another operation x13, other arithmetic, factor(): lower = jnp.linalg.cholesky(gram)  68.7 us
    another operation x5, other arithmetic, factor(): lax.linalg.triangular_solve(lower, identity, left_side=True, lower=True)  39.4 us
    dot_general x2, matrix products, gram_of(): lax.dot_general(flattened, flattened, (((0,), (0,)), ((), ())), precision...  33.5 us
    dot_general x3, matrix products, apply_inverse(): jnp.dot(flattened, inverse.T, precision=lax.Precision.HIGHEST, preferred_...  27.2 us
    ppermute x6, starting transfers between devices, reduce_gram(): y = y + lax.ppermute(y, 'rows', _xor_pairs(n_rows, bit))  9.14 us
  transfers between devices with their start and end apart: 14, of which 12 were waited for; matrix products, arithmetic and copies ran while one was open for 46% of the time, Pallas kernels for 0%

profile of v1, /device:TPU:0, one launch (start us, length us, event | category | flops | bytes accessed | tf_op | source)
XLA Modules:
  0.0 425.0 jit_solution(5530763650332512441)
XLA Ops:
  6.0 7.3 %all-to-all-start = ((s32[8,8,1]{1,2,0:T(1,128)}), s32[8,8,1]{1,2,0:T(1,128)S(1)}, u32[]{:S(2)}, u32[]{:S(2)}) async-start(s32[8,8,1]{1,2,0:T(1,128)} %bitcast.5), calls=%async_computation | async-start | bytes 8192 | tf_op jit(solution)/shard_map/all_to_all | solution.py:97
  13.3 7.7 %gather_fusion.1 = f32[64,128,256]{2,1,0:T(8,128)} fusion(f32[64,128,256]{2,1,0:T(8,128)} %bitcast.110, s32[1024]{0:T(1024)S(1)} %pad_clamp_fusion.1), kind=kCustom, calls=%fused_computation.1 | custom fusion | bytes 16777472 | tf_op jit(solution)/shard_map/jit(_take)/gather | solution.py:95
  21.0 8.3 %broadcast_select_fusion = f32[64,128,256]{2,1,0:T(8,128)} fusion(f32[64,128,256]{2,1,0:T(8,128)} %gather_fusion.1, pred[64]{0:T(512)(128)(4,1)S(1)} %compare_and_fusion), kind=kLoop, calls=%fused_computation.13 | loop fusion | flops 2097152 | bytes 16777280 | tf_op jit(solution)/shard_map/jit(_take)/select_n | solution.py:95
  29.3 6.0 %all-to-all-start.1 = ((f32[64,128,256]{2,1,0:T(8,128)}), f32[64,128,256]{2,1,0:T(8,128)}, u32[]{:S(2)}, u32[]{:S(2)}) async-start(f32[64,128,256]{2,1,0:T(8,128)} %broadcast_select_fusion), calls=%async_computation.1 | async-start | bytes 16777216 | tf_op jit(solution)/shard_map/all_to_all | solution.py:96
  35.3 19.7 %fusion.8 = f32[256,256]{0,1:T(8,128)S(1)} fusion(f32[64,1,128,256]{3,2,1,0:T(8,128)} %param.6, pred[64]{0:T(512)(128)(4,1)S(1)} %iota_compare_fusion.6), kind=kOutput, calls=%fused_computation.17 | convolution fusion | flops 6444613632 | bytes 8650816 | tf_op jit(solution)/shard_map/dot_general | solution.py:18
  58.2 4.0 collective-permute-done.1
  62.3 2.1 collective-permute-start.2
  64.4 42.0 %collective-permute-done.2 = f32[128,256]{0,1:T(8,128)S(1)} collective-permute-done((f32[128,256]{0,1:T(8,128)S(1)}, f32[128,256]{0,1:T(8,128)S(1)}, u32[]{:S(2)}, u32[]{:S(2)}) %collective-permute-start.2) | collective-permute-done | bytes 131104 | tf_op jit(solution)/shard_map/ppermute | solution.py:59
  107.0 66.3 %collective-permute-done.3 = f32[128,256]{0,1:T(8,128)S(1)} collective-permute-done((f32[128,256]{0,1:T(8,128)S(1)}, f32[128,256]{0,1:T(8,128)S(1)}, u32[]{:S(2)}, u32[]{:S(2)}) %collective-permute-start.3) | collective-permute-done | bytes 131104 | tf_op jit(solution)/shard_map/ppermute | solution.py:59
  173.4 4.0 collective-permute-start.4
  177.3 7.6 %bitcast_select_fusion = f32[8192,256]{1,0:T(8,128)} fusion(f32[64,1,128,256]{3,2,1,0:T(8,128)} %param.6, pred[8192]{0:T(1024)(128)(4,1)S(1)} %broadcast_bitcast_fusion), kind=kLoop, calls=%fused_computation.7 | loop fusion | flops 2097152 | bytes 16785408 | tf_op jit(solution)/shard_map/jit(_where)/select_n | solution.py:99
  185.0 38.4 %collective-permute-done.4 = f32[128,256]{0,1:T(8,128)S(1)} collective-permute-done((f32[128,256]{0,1:T(8,128)S(1)}, f32[128,256]{0,1:T(8,128)S(1)}, u32[]{:S(2)}, u32[]{:S(2)}) %collective-permute-start.4) | collective-permute-done | bytes 131104 | tf_op jit(solution)/shard_map/ppermute | solution.py:59
  225.1 11.7 %cholesky.130 = f32[128,128]{1,0:T(8,128)S(1)} custom-call(f32[128,128]{1,0:T(8,128)S(1)} %cholesky.194), custom_call_target="Cholesky" | custom-call | tf_op jit(solution)/shard_map/jit(cholesky)/cholesky | solution.py:10
  236.9 9.8 %custom-call.13 = f32[1,128,128]{1,2,0:T(8,128)S(1)} custom-call(f32[1,128,128]{2,1,0:T(8,128)S(1)} %get-tuple-element.59), custom_call_target="InvertDiagBlocksLowerTriangular" | custom-call | tf_op jit(solution)/shard_map/jit(cholesky)/cholesky | solution.py:10
  247.2 11.7 %cholesky.147 = f32[128,128]{1,0:T(8,128)S(1)} custom-call(f32[128,128]{1,0:T(8,128)S(1)} %convolution_subtract_fusion.3), custom_call_target="Cholesky" | custom-call | tf_op jit(solution)/shard_map/jit(cholesky)/cholesky | solution.py:10
  260.9 3.8 while.4
  264.7 19.7 %custom-call.14 = f32[2,128,128]{1,2,0:T(8,128)S(1)} custom-call(f32[2,128,128]{2,1,0:T(8,128)S(1)} %get-tuple-element.18), custom_call_target="InvertDiagBlocksLowerTriangular" | custom-call | tf_op jit(solution)/shard_map/triangular_solve/custom-call.0 | solution.py:12
  285.3 18.4 %fusion.23 = f32[8192,256]{1,0:T(8,128)S(1)} fusion(f32[8192,256]{1,0:T(8,128)} %bitcast_select_fusion, f32[128,256]{1,0:T(8,128)S(1)} %fusion.38, f32[128,256]{1,0:T(8,128)S(1)} %fusion.31), kind=kOutput, calls=%fused_computation.41 | convolution fusion | flops 6442516480 | bytes 17039360 | tf_op jit(solution)/shard_map/dot_general | solution.py:30
  303.7 13.8 %convolution_multiply_fusion = f32[256,256]{0,1:T(8,128)S(1)} fusion(f32[8192,256]{1,0:T(8,128)S(1)} %fusion.23), kind=kOutput, calls=%fused_computation.15 | convolution fusion | flops 6442516480 | bytes 8650752 | tf_op jit(solution)/shard_map/dot_general | solution.py:18
  320.7 4.1 collective-permute-done.7
  327.7 2.1 collective-permute-done.8
  329.9 4.9 %collective-permute-done.9 = f32[128,256]{0,1:T(8,128)S(1)} collective-permute-done((f32[128,256]{0,1:T(8,128)S(1)}, f32[128,256]{0,1:T(8,128)S(1)}, u32[]{:S(2)}, u32[]{:S(2)}) %collective-permute-start.9) | collective-permute-done | bytes 131104 | tf_op jit(solution)/shard_map/ppermute | solution.py:59
  335.8 5.8 %collective-permute-done.10 = f32[128,256]{0,1:T(8,128)S(1)} collective-permute-done((f32[128,256]{0,1:T(8,128)S(1)}, f32[128,256]{0,1:T(8,128)S(1)}, u32[]{:S(2)}, u32[]{:S(2)}) %collective-permute-start.10) | collective-permute-done | bytes 131104 | tf_op jit(solution)/shard_map/ppermute | solution.py:59
  343.3 11.7 %cholesky.164 = f32[128,128]{1,0:T(8,128)S(1)} custom-call(f32[128,128]{1,0:T(8,128)S(1)} %cholesky.197), custom_call_target="Cholesky" | custom-call | tf_op jit(solution)/shard_map/jit(cholesky)/cholesky | solution.py:10
  355.1 9.8 %custom-call.15 = f32[1,128,128]{1,2,0:T(8,128)S(1)} custom-call(f32[1,128,128]{2,1,0:T(8,128)S(1)} %get-tuple-element.55), custom_call_target="InvertDiagBlocksLowerTriangular" | custom-call | tf_op jit(solution)/shard_map/jit(cholesky)/cholesky | solution.py:10
  365.4 11.9 %cholesky.181 = f32[128,128]{1,0:T(8,128)S(1)} custom-call(f32[128,128]{1,0:T(8,128)S(1)} %convolution_subtract_fusion.2), custom_call_target="Cholesky" | custom-call | tf_op jit(solution)/shard_map/jit(cholesky)/cholesky | solution.py:10
  379.8 3.8 while.5
  383.7 19.7 %custom-call.16 = f32[2,128,128]{1,2,0:T(8,128)S(1)} custom-call(f32[2,128,128]{2,1,0:T(8,128)S(1)} %get-tuple-element.19), custom_call_target="InvertDiagBlocksLowerTriangular" | custom-call | tf_op jit(solution)/shard_map/triangular_solve/custom-call.0 | solution.py:12
  405.5 6.2 %gather_fusion.2 = f32[32,128,256]{2,1,0:T(8,128)} fusion(f32[64,128,256]{2,1,0:T(8,128)} %all-to-all-done.1, s32[1024]{0:T(1024)S(1)} %pad_clamp_fusion), kind=kCustom, calls=%fused_computation.2 | custom fusion | bytes 8388736 | tf_op jit(solution)/shard_map/jit(_take)/gather | solution.py:107
  411.7 4.1 bitcast_select_fusion.1
  415.8 3.8 fusion.24
  419.5 5.0 %fusion.11 = f32[4096,256]{1,0:T(8,128)} fusion(f32[4096,256]{1,0:T(8,128)S(1)} %fusion.24, f32[128,256]{1,0:T(8,128)S(1)} %fusion.34, f32[128,256]{1,0:T(8,128)S(1)} %fusion.29), kind=kOutput, calls=%fused_computation.25 | convolution fusion | flops 3221291008 | bytes 8650752 | tf_op jit(solution)/shard_map/dot_general | solution.py:30
  (100 shorter events, 32.7 us)
Async XLA Ops:
  6.0 23.3 %all-to-all-start = ((s32[8,8,1]{1,2,0:T(1,128)}), s32[8,8,1]{1,2,0:T(1,128)S(1)}, u32[]{:S(2)}, u32[]{:S(2)}) async-start(s32[8,8,1]{1,2,0:T(1,128)} %bitcast.5), calls=%async_computation | async-start | bytes 8192 | tf_op jit(solution)/shard_map/all_to_all | solution.py:97
  29.3 376.2 %all-to-all-start.1 = ((f32[64,128,256]{2,1,0:T(8,128)}), f32[64,128,256]{2,1,0:T(8,128)}, u32[]{:S(2)}, u32[]{:S(2)}) async-start(f32[64,128,256]{2,1,0:T(8,128)} %broadcast_select_fusion), calls=%async_computation.1 | async-start | bytes 16777216 | tf_op jit(solution)/shard_map/all_to_all | solution.py:96
  55.0 1.6 collective-permute-start
  56.7 5.6 %collective-permute-start.1 = (f32[128,256]{0,1:T(8,128)S(1)}, f32[128,256]{0,1:T(8,128)S(1)}, u32[]{:S(2)}, u32[]{:S(2)}) collective-permute-start(f32[128,256]{0,1:T(8,128)S(1)} %dynamic-slice_add_fusion.1), channel_id=1, source_target_pairs={{0,2},{1,3},{2,0},{3,1},{4,6},{5,7},{6,4},{7,5},{8,10},{9,11},{10,... | collective-permute-start | bytes 393224 | tf_op jit(solution)/shard_map/ppermute | solution.py:55
  62.3 44.0 %collective-permute-start.2 = (f32[128,256]{0,1:T(8,128)S(1)}, f32[128,256]{0,1:T(8,128)S(1)}, u32[]{:S(2)}, u32[]{:S(2)}) collective-permute-start(f32[128,256]{0,1:T(8,128)S(1)} %add.146), channel_id=1, source_target_pairs={{0,4},{4,0},{8,12},{12,8},{16,20},{20,16},{24,28},{28,24},{1,5},{5... | collective-permute-start | bytes 393224 | tf_op jit(solution)/shard_map/ppermute | solution.py:59
  106.3 67.0 %collective-permute-start.3 = (f32[128,256]{0,1:T(8,128)S(1)}, f32[128,256]{0,1:T(8,128)S(1)}, u32[]{:S(2)}, u32[]{:S(2)}) collective-permute-start(f32[128,256]{0,1:T(8,128)S(1)} %add.147), channel_id=1, source_target_pairs={{0,8},{4,12},{8,0},{12,4},{16,24},{20,28},{24,16},{28,20},{1,9},{5... | collective-permute-start | bytes 393224 | tf_op jit(solution)/shard_map/ppermute | solution.py:59
  173.4 50.0 %collective-permute-start.4 = (f32[128,256]{0,1:T(8,128)S(1)}, f32[128,256]{0,1:T(8,128)S(1)}, u32[]{:S(2)}, u32[]{:S(2)}) collective-permute-start(f32[128,256]{0,1:T(8,128)S(1)} %add.148), channel_id=1, source_target_pairs={{0,16},{4,20},{8,24},{12,28},{16,0},{20,4},{24,8},{28,12},{1,17},{... | collective-permute-start | bytes 393224 | tf_op jit(solution)/shard_map/ppermute | solution.py:59
  223.4 1.4 collective-permute-start.5
  317.5 1.6 collective-permute-start.6
  319.1 5.6 %collective-permute-start.7 = (f32[128,256]{0,1:T(8,128)S(1)}, f32[128,256]{0,1:T(8,128)S(1)}, u32[]{:S(2)}, u32[]{:S(2)}) collective-permute-start(f32[128,256]{0,1:T(8,128)S(1)} %dynamic-slice_add_fusion), channel_id=1, source_target_pairs={{0,2},{1,3},{2,0},{3,1},{4,6},{5,7},{6,4},{7,5},{8,10},{9,11},{10,... | collective-permute-start | bytes 393224 | tf_op jit(solution)/shard_map/ppermute | solution.py:55
  324.8 5.0 %collective-permute-start.8 = (f32[128,256]{0,1:T(8,128)S(1)}, f32[128,256]{0,1:T(8,128)S(1)}, u32[]{:S(2)}, u32[]{:S(2)}) collective-permute-start(f32[128,256]{0,1:T(8,128)S(1)} %add.151), channel_id=1, source_target_pairs={{0,4},{4,0},{8,12},{12,8},{16,20},{20,16},{24,28},{28,24},{1,5},{5... | collective-permute-start | bytes 393224 | tf_op jit(solution)/shard_map/ppermute | solution.py:59
  329.8 5.0 %collective-permute-start.9 = (f32[128,256]{0,1:T(8,128)S(1)}, f32[128,256]{0,1:T(8,128)S(1)}, u32[]{:S(2)}, u32[]{:S(2)}) collective-permute-start(f32[128,256]{0,1:T(8,128)S(1)} %add.152), channel_id=1, source_target_pairs={{0,8},{4,12},{8,0},{12,4},{16,24},{20,28},{24,16},{28,20},{1,9},{5... | collective-permute-start | bytes 393224 | tf_op jit(solution)/shard_map/ppermute | solution.py:59
  334.9 6.8 %collective-permute-start.10 = (f32[128,256]{0,1:T(8,128)S(1)}, f32[128,256]{0,1:T(8,128)S(1)}, u32[]{:S(2)}, u32[]{:S(2)}) collective-permute-start(f32[128,256]{0,1:T(8,128)S(1)} %add.153), channel_id=1, source_target_pairs={{0,16},{4,20},{8,24},{12,28},{16,0},{20,4},{24,8},{28,12},{1,17},{... | collective-permute-start | bytes 393224 | tf_op jit(solution)/shard_map/ppermute | solution.py:59
  341.7 1.4 collective-permute-start.11
